TPU v7x, 32 devices: a whole 2x2x4 slice. The times are simulated.
32 devices in a mesh: tile: 8 (over z, core), deg: 4 (over y, x).
Axes of the slice: x: 2, y: 2, z: 4, core: 2. Of those that a mesh axis runs over, the one named last changes fastest.
Arguments:
- field: float32 [3, 8, 128, 512], P(None, None, 'tile', 'deg'), may hold values from -6 to 6
- flow: float32 [3, 8, 128, 512], P(None, None, 'tile', 'deg'), may hold values from -3 to 3
- match_ops: bfloat16 [32, 512, 512], P(('tile', 'deg')), may hold values from -0.5 to 20.5
- wave_of_slot: int32 [32], replicated, may hold values from 0 to 31, each once
Outputs:
- advanced: float32 [3, 8, 128, 512], P(None, None, 'tile', 'deg')
Inputs may be any that keep to these rules, and one draw needn't show every extreme that they name: `wave_of_slot`: every wavenumber from 0 to 31 is named by exactly one slot.
All inputs are finite; a program needn't handle non-finite values.
Results may differ from a plain program's by a relative error of at most 0.00065.
Values may be sent and summed in bfloat16 or wider, within the bound.
No kernel may reach another device: no remote copies, remote signals or barrier semaphores. Data moves between devices by JAX's collectives and lax.ppermute only.
A program may use at most 64 MiB of HBM per device.

v0:
```python
import math
import jax
import jax.numpy as jnp
from jax import lax
from jax.sharding import PartitionSpec as P

P_SIZE = 8
diffusivity = 0.05
time_step = 0.01
highest = lax.Precision.HIGHEST
gll_interior = [0.2092992179024789, 0.5917001814331423, 0.8717401485096066]


def padded_2(value, sides, width):
    for axis, dim in sides:
        size, length = (lax.axis_size(axis), value.shape[dim])
        up = [(i, (i + 1) % size) for i in range(size)]
        down = [(j, i) for i, j in up]
        last = lax.slice_in_dim(value, length - width, length, axis=dim)
        first = lax.slice_in_dim(value, 0, width, axis=dim)
        before = lax.ppermute(last, axis, up)
        after = lax.ppermute(first, axis, down)
        value = jnp.concatenate([before, value, after], axis=dim)
    return value


def legendre_value(point, degree):
    previous = 1.0
    current = point
    for order in range(1, degree):
        following = ((2 * order + 1) * point * current - order * previous) / (order + 1)
        previous = current
        current = following
    return current


def gll_tables(count):
    degree = count - 1
    points = [-1.0] + [-value for value in reversed(gll_interior)] + list(gll_interior) + [1.0]
    values = [legendre_value(point, degree) for point in points]
    weights = [2.0 / (degree * (degree + 1) * value * value) for value in values]
    matrix = [
        [
            values[row] / (values[col] * (points[row] - points[col])) if row != col else 0.0
            for col in range(count)
        ]
        for row in range(count)
    ]
    matrix[0][0] = -degree * (degree + 1) / 4.0
    matrix[count - 1][count - 1] = degree * (degree + 1) / 4.0
    return (points, weights, matrix)


def apply_along(values, axis_pos, matrix):
    shape = values.shape
    blocks = values.reshape(
        shape[:axis_pos] + (shape[axis_pos] // P_SIZE, P_SIZE) + shape[axis_pos + 1 :]
    )
    letters = list("abcdefg"[: blocks.ndim])
    source = list(letters)
    source[axis_pos + 1] = "p"
    target = list(letters)
    target[axis_pos + 1] = "q"
    formula = "".join(source) + ",qp->" + "".join(target)
    return jnp.einsum(formula, blocks, matrix, precision=highest).reshape(shape)


def assemble_dim(values, axis_pos, left, right):
    shape = values.shape
    count = shape[axis_pos] // P_SIZE
    blocks = values.reshape(shape[:axis_pos] + (count, P_SIZE) + shape[axis_pos + 1 :])
    edge_shape = shape[:axis_pos] + (1, 1) + shape[axis_pos + 1 :]
    first = lax.slice_in_dim(blocks, 0, 1, axis=axis_pos + 1)
    last = lax.slice_in_dim(blocks, P_SIZE - 1, P_SIZE, axis=axis_pos + 1)
    before = jnp.concatenate(
        [left.reshape(edge_shape), lax.slice_in_dim(last, 0, count - 1, axis=axis_pos)],
        axis=axis_pos,
    )
    after = jnp.concatenate(
        [lax.slice_in_dim(first, 1, count, axis=axis_pos), right.reshape(edge_shape)], axis=axis_pos
    )
    middle = lax.slice_in_dim(blocks, 1, P_SIZE - 1, axis=axis_pos + 1)
    joined = jnp.concatenate([first + before, middle, last + after], axis=axis_pos + 1)
    return joined.reshape(shape)


def assembled_weights(weights, count, lead, trail):
    position = jnp.arange(count * P_SIZE, dtype=jnp.int32)
    local_point = position % P_SIZE
    element = position // P_SIZE
    base = jnp.tile(weights, count)
    starts = (
        jnp.where(local_point == 0, jnp.where(element > 0, 1.0, lead), 0.0) * weights[P_SIZE - 1]
    )
    ends = (
        jnp.where(local_point == P_SIZE - 1, jnp.where(element < count - 1, 1.0, trail), 0.0)
        * weights[0]
    )
    return base + starts + ends


def phases(waves, elem_start, elem_count, span, points):
    element = elem_start + jnp.arange(elem_count * P_SIZE, dtype=jnp.int32) // P_SIZE
    whole = waves[:, None] * (2 * element + 1)[None, :] % span
    fraction = waves.astype(jnp.float32)[:, None] * jnp.tile(points, elem_count)[None, :]
    return 2.0 * math.pi / span * (whole.astype(jnp.float32) + fraction)


def local(field, flow, match_ops, wave_of_slot):
    tiles = lax.axis_size("tile")
    groups = lax.axis_size("deg")
    tile_index = lax.axis_index("tile")
    group_index = lax.axis_index("deg")
    radial_nodes = field.shape[1]
    na_dev = field.shape[2]
    nb_dev = field.shape[3]
    elems_a = na_dev // P_SIZE
    elems_b = nb_dev // P_SIZE
    span = 2 * elems_a * tiles
    per_tile = wave_of_slot.shape[0] // tiles
    scale = P_SIZE / (na_dev * tiles)
    points_list, weights_list, matrix_list = gll_tables(P_SIZE)
    points = jnp.asarray(points_list, jnp.float32)
    weights = jnp.asarray(weights_list, jnp.float32)
    dmat = jnp.asarray(matrix_list, jnp.float32)
    block = jnp.kron(jnp.eye(elems_b, dtype=jnp.float32), dmat)
    lead = (group_index > 0).astype(jnp.float32)
    trail = (group_index < groups - 1).astype(jnp.float32)
    w_r = jnp.tile(weights, radial_nodes // P_SIZE)
    w_a = jnp.tile(weights, elems_a)
    w_b = jnp.tile(weights, elems_b)
    mass3 = w_r[:, None, None] * w_a[None, :, None] * w_b[None, None, :]
    surface_weight = w_a[:, None] * w_b[None, :]
    assembled = (
        assembled_weights(weights, radial_nodes // P_SIZE, 0.0, 0.0)[:, None, None]
        * assembled_weights(weights, elems_a, 1.0, 1.0)[None, :, None]
        * assembled_weights(weights, elems_b, lead, trail)[None, None, :]
    )
    column_mask = jnp.concatenate([lead[None], jnp.ones((nb_dev,), jnp.float32), trail[None]])

    def derive(values, direction, transpose):
        if direction == 2:
            table = block if transpose else block.T
            return jnp.dot(values, table, precision=highest)
        return apply_along(values, direction, dmat.T if transpose else dmat)

    flow_parts = [flow[0], flow[1], flow[2]]
    grad_flow = [
        [derive(flow_parts[component], direction, False) for direction in range(3)]
        for component in range(3)
    ]

    def analyse(surface):
        angle = phases(wave_of_slot, tile_index * elems_a, elems_a, span, points)
        table = (
            jnp.stack([jnp.cos(angle), jnp.sin(angle)], axis=1) * (w_a * scale)[None, None, :]
        ).reshape(lax.axis_size("tile") * per_tile * 2, na_dev)
        return jnp.dot(table, surface, precision=highest).reshape(
            lax.axis_size("tile") * per_tile, 2, nb_dev
        )

    def surface_flux(surface):
        coeff = lax.psum_scatter(analyse(surface), "tile", scatter_dimension=0, tiled=True)
        owned = lax.all_to_all(
            coeff.astype(jnp.bfloat16), "deg", split_axis=0, concat_axis=2, tiled=True
        )
        mapped = jnp.einsum("kpq,kcq->kcp", match_ops, owned, preferred_element_type=jnp.float32)
        matched = lax.all_to_all(mapped, "deg", split_axis=2, concat_axis=0, tiled=True)
        my_waves = lax.dynamic_slice_in_dim(wave_of_slot, tile_index * per_tile, per_tile)
        flat_matched = matched.reshape(per_tile * 2, nb_dev)
        angle = phases(
            my_waves, jnp.int32(0) // P_SIZE, lax.axis_size("tile") * na_dev // P_SIZE, span, points
        )
        table = jnp.stack([jnp.cos(angle).T, jnp.sin(angle).T], axis=2).reshape(
            lax.axis_size("tile") * na_dev, per_tile * 2
        )
        total = lax.psum_scatter(
            jnp.dot(table, flat_matched, precision=highest), "tile", scatter_dimension=0, tiled=True
        )
        return -total

    def tendency(parts):
        rhs = []
        for component in range(3):
            slopes = [derive(parts[component], direction, False) for direction in range(3)]
            stretch = (
                parts[0] * grad_flow[component][0]
                + parts[1] * grad_flow[component][1]
                + parts[2] * grad_flow[component][2]
            )
            carried = (
                flow_parts[0] * slopes[0] + flow_parts[1] * slopes[1] + flow_parts[2] * slopes[2]
            )
            spread = (
                derive(mass3 * slopes[0], 0, True)
                + derive(mass3 * slopes[1], 1, True)
                + derive(mass3 * slopes[2], 2, True)
            )
            rhs.append(mass3 * (stretch - carried) - diffusivity * spread)
        flux = surface_flux(parts[0][radial_nodes - 1])
        rhs[0] = rhs[0].at[radial_nodes - 1].add(diffusivity * surface_weight * flux)
        stacked = jnp.stack(rhs)
        plane_r = jnp.zeros_like(lax.slice_in_dim(stacked, 0, 1, axis=1))
        stacked = assemble_dim(stacked, 1, plane_r, plane_r)
        padded = padded_2(stacked.astype(jnp.bfloat16), (("tile", 2), ("deg", 3)), 1).astype(
            stacked.dtype
        )
        padded = padded * column_mask
        along_a = assemble_dim(padded[:, :, 1:-1, :], 2, padded[:, :, 0:1, :], padded[:, :, -1:, :])
        along_b = assemble_dim(
            along_a[:, :, :, 1:-1], 3, along_a[:, :, :, 0:1], along_a[:, :, :, -1:]
        )
        return along_b / assembled[None]

    section = field + time_step * tendency([field[0], field[1], field[2]])
    return 0.5 * (field + section + time_step * tendency([section[0], section[1], section[2]]))


def solution(mesh):
    placed = (
        P(None, None, "tile", "deg"),
        P(None, None, "tile", "deg"),
        P(("tile", "deg"), None, None),
        P(),
    )
    return jax.shard_map(
        local, mesh=mesh, in_specs=placed, out_specs=P(None, None, "tile", "deg"), check_vma=False
    )
```

profile of v0, /device:TPU:0, one launch (start us, length us, event | category | flops | bytes accessed | tf_op | source)
XLA Modules:
  0.0 227.2 jit_solution(8538211180107501560)
XLA Ops:
  10.2 1.0 fusion.116
  11.2 30.3 %all-reduce = bf16[32,2,128]{2,0,1:T(8,128)(2,1)S(1)} all-reduce(f32[32,2,128]{2,0,1:T(8,128)S(1)} %fusion.116), channel_id=2, replica_groups=mesh['tile'=8,'deg'=4] {'tile'}, use_global_device_ids=true, to_apply=%region_0.1.clone | all-reduce | flops 8192 | bytes 49152
  41.5 1.2 dynamic-slice.16
  43.9 3.7 %all-to-all-start = ((bf16[4,2,128]{2,1,0:T(2,128)(2,1)}), bf16[4,2,128]{2,1,0:T(2,128)(2,1)S(1)}, u32[]{:S(2)}, u32[]{:S(2)}) async-start(bf16[4,2,128]{2,1,0:T(2,128)(2,1)} %copy.334), calls=%async_computation | async-start | bytes 4096 | tf_op jit(solution)/shard_map/all_to_all | solution.py:164
  49.4 1.1 fusion.51
  50.5 1.0 convolution_bitcast_fusion.6
  51.6 0.9 fusion.169
  53.3 1.0 fusion.54
  62.6 1.2 reduce.4
  64.6 4.2 %all-to-all-start.1 = ((f32[4,1,256]{2,1,0:T(1,128)}), f32[4,1,256]{2,1,0:T(1,128)S(1)}, u32[]{:S(2)}, u32[]{:S(2)}) async-start(f32[4,1,256]{2,1,0:T(1,128)} %reshape.1012), calls=%async_computation.1 | async-start | bytes 8192 | tf_op jit(solution)/shard_map/all_to_all | solution.py:168
  68.8 4.7 %all-to-all-done.1 = f32[4,1,256]{2,1,0:T(1,128)S(1)} async-done(((f32[4,1,256]{2,1,0:T(1,128)}), f32[4,1,256]{2,1,0:T(1,128)S(1)}, u32[]{:S(2)}, u32[]{:S(2)}) %all-to-all-start.1) | async-done | bytes 4128 | tf_op jit(solution)/shard_map/all_to_all | solution.py:168
  76.1 25.9 %reduce-scatter.5.cloned.1.call-done = f32[16,128]{1,0:T(8,128)} async-done(((f32[128,128]{1,0:T(8,128)}), f32[16,128]{1,0:T(8,128)}) %reduce-scatter.5.cloned.1.call-update) | async-done | bytes 8208 | tf_op jit(solution)/shard_map/reduce_scatter | solution.py:177
  104.4 3.5 %collective-permute-done = bf16[3,8,1,128]{3,1,2,0:T(8,128)(2,1)S(1)} collective-permute-done((bf16[3,8,1,128]{3,1,2,0:T(8,128)(2,1)S(1)}, bf16[3,8,1,128]{3,1,2,0:T(8,128)(2,1)S(1)}, u32[]{:S(2)}, u32[]{:S(2)}) %collective-permute-start) | collective-permute-done | bytes 6176 | tf_op jit(solution)/shard_map/ppermute | solution.py:21
  108.0 2.7 %collective-permute-start.3 = (bf16[3,8,18,1]{3,1,2,0:T(8,128)(2,1)S(1)}, bf16[3,8,18,1]{3,1,2,0:T(8,128)(2,1)S(1)}, u32[]{:S(2)}, u32[]{:S(2)}) collective-permute-start(bf16[3,8,18,1]{3,1,2,0:T(8,128)(2,1)S(1)} %get-tuple-element.73), channel_id=1, source_target_pairs={{1,0},{2,1},{3,2},{0,3},{5,4},{6,5},{7,6},{4,7},{9,8},{10,9},{11,1... | collective-permute-start | bytes 2600 | tf_op jit(solution)/shard_map/ppermute | solution.py:22
  110.8 2.2 collective-permute-done.3
  113.0 3.3 %collective-permute-done.2 = bf16[3,8,18,1]{3,1,2,0:T(8,128)(2,1)S(1)} collective-permute-done((bf16[3,8,18,1]{3,1,2,0:T(8,128)(2,1)S(1)}, bf16[3,8,18,1]{3,1,2,0:T(8,128)(2,1)S(1)}, u32[]{:S(2)}, u32[]{:S(2)}) %collective-permute-start.2) | collective-permute-done | bytes 896 | tf_op jit(solution)/shard_map/ppermute | solution.py:21
  117.7 1.3 slice.297
  120.0 2.0 maximum_bitcast_fusion
  126.1 26.0 %all-reduce.1 = bf16[32,2,128]{2,0,1:T(8,128)(2,1)S(1)} all-reduce(f32[32,2,128]{2,0,1:T(8,128)S(1)} %fusion.115), channel_id=4, replica_groups=mesh['tile'=8,'deg'=4] {'tile'}, use_global_device_ids=true, to_apply=%region_2.3.clone | all-reduce | flops 8192 | bytes 49152
  152.7 3.2 %all-to-all-start.2 = ((bf16[4,2,128]{2,1,0:T(2,128)(2,1)}), bf16[4,2,128]{2,1,0:T(2,128)(2,1)S(1)}, u32[]{:S(2)}, u32[]{:S(2)}) async-start(bf16[4,2,128]{2,1,0:T(2,128)(2,1)} %copy.387), calls=%async_computation.3 | async-start | bytes 4096 | tf_op jit(solution)/shard_map/all_to_all | solution.py:164
  156.9 3.5 %all-to-all-done.2 = bf16[4,2,128]{2,1,0:T(2,128)(2,1)S(1)} async-done(((bf16[4,2,128]{2,1,0:T(2,128)(2,1)}), bf16[4,2,128]{2,1,0:T(2,128)(2,1)S(1)}, u32[]{:S(2)}, u32[]{:S(2)}) %all-to-all-start.2) | async-done | bytes 2080 | tf_op jit(solution)/shard_map/all_to_all | solution.py:164
  160.7 1.2 reduce.6
  162.7 3.2 %all-to-all-start.3 = ((f32[4,1,256]{2,1,0:T(1,128)}), f32[4,1,256]{2,1,0:T(1,128)S(1)}, u32[]{:S(2)}, u32[]{:S(2)}) async-start(f32[4,1,256]{2,1,0:T(1,128)} %reshape.1014), calls=%async_computation.4 | async-start | bytes 8192 | tf_op jit(solution)/shard_map/all_to_all | solution.py:168
  166.3 4.3 %all-to-all-done.3 = f32[4,1,256]{2,1,0:T(1,128)S(1)} async-done(((f32[4,1,256]{2,1,0:T(1,128)}), f32[4,1,256]{2,1,0:T(1,128)S(1)}, u32[]{:S(2)}, u32[]{:S(2)}) %all-to-all-start.3) | async-done | bytes 4128 | tf_op jit(solution)/shard_map/all_to_all | solution.py:168
  172.9 26.3 %reduce-scatter.7.cloned.1.call-done = f32[16,128]{1,0:T(8,128)} async-done(((f32[128,128]{1,0:T(8,128)}), f32[16,128]{1,0:T(8,128)}) %reduce-scatter.7.cloned.1.call-update) | async-done | bytes 8208 | tf_op jit(solution)/shard_map/reduce_scatter | solution.py:177
  200.6 0.9 collective-permute-done.5
  201.6 3.5 %collective-permute-done.4 = bf16[3,8,1,128]{3,1,2,0:T(8,128)(2,1)S(1)} collective-permute-done((bf16[3,8,1,128]{3,1,2,0:T(8,128)(2,1)S(1)}, bf16[3,8,1,128]{3,1,2,0:T(8,128)(2,1)S(1)}, u32[]{:S(2)}, u32[]{:S(2)}) %collective-permute-start.4) | collective-permute-done | bytes 6176 | tf_op jit(solution)/shard_map/ppermute | solution.py:21
  205.2 2.7 %collective-permute-start.7 = (bf16[3,8,18,1]{3,1,2,0:T(8,128)(2,1)S(1)}, bf16[3,8,18,1]{3,1,2,0:T(8,128)(2,1)S(1)}, u32[]{:S(2)}, u32[]{:S(2)}) collective-permute-start(bf16[3,8,18,1]{3,1,2,0:T(8,128)(2,1)S(1)} %get-tuple-element.71), channel_id=1, source_target_pairs={{1,0},{2,1},{3,2},{0,3},{5,4},{6,5},{7,6},{4,7},{9,8},{10,9},{11,1... | collective-permute-start | bytes 2600 | tf_op jit(solution)/shard_map/ppermute | solution.py:22
  207.9 2.3 %collective-permute-done.7 = bf16[3,8,18,1]{3,1,2,0:T(8,128)(2,1)S(1)} collective-permute-done((bf16[3,8,18,1]{3,1,2,0:T(8,128)(2,1)S(1)}, bf16[3,8,18,1]{3,1,2,0:T(8,128)(2,1)S(1)}, u32[]{:S(2)}, u32[]{:S(2)}) %collective-permute-start.7) | collective-permute-done | bytes 896 | tf_op jit(solution)/shard_map/ppermute | solution.py:22
  210.2 3.3 %collective-permute-done.6 = bf16[3,8,18,1]{3,1,2,0:T(8,128)(2,1)S(1)} collective-permute-done((bf16[3,8,18,1]{3,1,2,0:T(8,128)(2,1)S(1)}, bf16[3,8,18,1]{3,1,2,0:T(8,128)(2,1)S(1)}, u32[]{:S(2)}, u32[]{:S(2)}) %collective-permute-start.6) | collective-permute-done | bytes 896 | tf_op jit(solution)/shard_map/ppermute | solution.py:21
  214.8 1.3 slice.320
  217.1 2.0 maximum_bitcast_fusion.1
  (224 shorter events, 36.4 us)
Async XLA Ops:
  6.5 55.3 %copy-start = (bf16[1,512,512]{2,1,0:T(8,128)(2,1)S(1)}, bf16[1,512,512]{2,1,0:T(8,128)(2,1)}, u32[]{:S(2)}) copy-start(bf16[1,512,512]{2,1,0:T(8,128)(2,1)} %param.13) | copy-start | bytes 1572868
  8.7 39.7 %copy-start.32 = (f32[16]{0:T(128)}, f32[16]{0:T(128)S(1)}, u32[]{:S(2)}) copy-start(f32[16]{0:T(128)S(1)} %get-tuple-element.95) | copy-start | bytes 196
  43.9 17.9 %all-to-all-start = ((bf16[4,2,128]{2,1,0:T(2,128)(2,1)}), bf16[4,2,128]{2,1,0:T(2,128)(2,1)S(1)}, u32[]{:S(2)}, u32[]{:S(2)}) async-start(bf16[4,2,128]{2,1,0:T(2,128)(2,1)} %copy.334), calls=%async_computation | async-start | bytes 4096 | tf_op jit(solution)/shard_map/all_to_all | solution.py:164
  48.5 12.3 %copy-start.24 = (f32[8,2,8]{2,1,0:T(2,128)}, f32[8,2,8]{2,1,0:T(2,128)S(1)}, u32[]{:S(2)}) copy-start(f32[8,2,8]{2,1,0:T(2,128)S(1)} %broadcast_multiply_fusion.3) | copy-start | bytes 1540
  49.4 6.3 %copy-start.2 = (f32[3,8,16,128]{3,2,1,0:T(8,128)S(1)}, f32[3,8,16,128]{3,2,1,0:T(8,128)}, u32[]{:S(2)}) copy-start(f32[3,8,16,128]{3,2,1,0:T(8,128)} %param.12) | copy-start | bytes 589828
  49.4 6.5 %copy-start.1 = (f32[3,8,16,128]{3,2,1,0:T(8,128)S(1)}, f32[3,8,16,128]{3,2,1,0:T(8,128)}, u32[]{:S(2)}) copy-start(f32[3,8,16,128]{3,2,1,0:T(8,128)} %param.11) | copy-start | bytes 589828
  51.6 7.2 %copy-start.10 = (f32[8,16,128]{2,1,0:T(8,128)}, f32[8,16,128]{2,1,0:T(8,128)S(1)}, u32[]{:S(2)}) copy-start(f32[8,16,128]{2,1,0:T(8,128)S(1)} %convolution_bitcast_fusion.6) | copy-start | bytes 196612
  51.6 4.9 %copy-start.22 = (f32[8,8,1,1]{1,0,3,2:T(8,128)S(1)}, f32[8,8,1,1]{1,0,3,2:T(8,128)}, u32[]{:S(2)}) copy-start(f32[8,8,1,1]{1,0,3,2:T(8,128)} %constant.239) | copy-start | bytes 772
  54.3 3.2 %copy-start.23 = (f32[8]{0:T(128)S(1)}, f32[8]{0:T(128)}, u32[]{:S(2)}) copy-start(f32[8]{0:T(128)} %constant.223.clone) | copy-start | bytes 100
  55.2 2.8 %copy-start.3 = (f32[8,8,1]{1,0,2:T(8,128)S(1)}, f32[8,8,1]{1,0,2:T(8,128)}, u32[]{:S(2)}) copy-start(f32[8,8,1]{1,0,2:T(8,128)} %constant.238) | copy-start | bytes 772
  56.0 3.1 %copy-start.4 = (f32[8,16,128]{2,1,0:T(8,128)}, f32[8,16,128]{2,1,0:T(8,128)S(1)}, u32[]{:S(2)}) copy-start(f32[8,16,128]{2,1,0:T(8,128)S(1)} %convolution_bitcast_fusion.5) | copy-start | bytes 196612
  56.5 19.0 %copy-start.6 = (f32[8,16,128]{2,1,0:T(8,128)}, f32[8,16,128]{2,1,0:T(8,128)S(1)}, u32[]{:S(2)}) copy-start(f32[8,16,128]{2,1,0:T(8,128)S(1)} %convolution_bitcast_fusion.9) | copy-start | bytes 196612
  57.0 3.0 %copy-start.31 = (f32[8]{0:T(128)S(1)}, f32[8]{0:T(128)}, u32[]{:S(2)}) copy-start(f32[8]{0:T(128)} %constant.222.clone) | copy-start | bytes 100
  57.0 3.1 %copy-start.30 = (s32[32]{0:T(128)S(1)}, s32[32]{0:T(128)}, u32[]{:S(2)}) copy-start(s32[32]{0:T(128)} %param.14) | copy-start | bytes 388
  57.3 4.0 %copy-start.8 = (f32[8,16,128]{2,1,0:T(8,128)}, f32[8,16,128]{2,1,0:T(8,128)S(1)}, u32[]{:S(2)}) copy-start(f32[8,16,128]{2,1,0:T(8,128)S(1)} %convolution_bitcast_fusion.13) | copy-start | bytes 196612
  57.5 3.8 %copy-start.12 = (f32[8,16,128]{2,1,0:T(8,128)}, f32[8,16,128]{2,1,0:T(8,128)S(1)}, u32[]{:S(2)}) copy-start(f32[8,16,128]{2,1,0:T(8,128)S(1)} %convolution_bitcast_fusion.14) | copy-start | bytes 196612
  58.4 2.7 %copy-start.14 = (f32[8,16,128]{2,0,1:T(8,128)}, f32[8,16,128]{2,0,1:T(8,128)S(1)}, u32[]{:S(2)}) copy-start(f32[8,16,128]{2,0,1:T(8,128)S(1)} %fusion.98) | copy-start | bytes 196612
  59.5 16.0 %copy-start.16 = (f32[8,16,128]{2,0,1:T(8,128)}, f32[8,16,128]{2,0,1:T(8,128)S(1)}, u32[]{:S(2)}) copy-start(f32[8,16,128]{2,0,1:T(8,128)S(1)} %fusion.84) | copy-start | bytes 196612
  61.8 14.1 %copy-start.20 = (f32[8,16,128]{2,1,0:T(8,128)}, f32[8,16,128]{2,1,0:T(8,128)S(1)}, u32[]{:S(2)}) copy-start(f32[8,16,128]{2,1,0:T(8,128)S(1)} %convolution_bitcast_fusion.10) | copy-start | bytes 196612
  64.6 8.9 %all-to-all-start.1 = ((f32[4,1,256]{2,1,0:T(1,128)}), f32[4,1,256]{2,1,0:T(1,128)S(1)}, u32[]{:S(2)}, u32[]{:S(2)}) async-start(f32[4,1,256]{2,1,0:T(1,128)} %reshape.1012), calls=%async_computation.1 | async-start | bytes 8192 | tf_op jit(solution)/shard_map/all_to_all | solution.py:168
  68.8 33.2 %reduce-scatter.5.cloned.1.call-start = ((), (), s32[]{:S(2)}) async-start(), calls=%async_computation.6 | async-start | bytes 73728 | tf_op jit(solution)/shard_map/reduce_scatter | solution.py:177
  102.8 1.5 collective-permute-start.1
  103.0 4.9 %collective-permute-start = (bf16[3,8,1,128]{3,1,2,0:T(8,128)(2,1)S(1)}, bf16[3,8,1,128]{3,1,2,0:T(8,128)(2,1)S(1)}, u32[]{:S(2)}, u32[]{:S(2)}) collective-permute-start(bf16[3,8,1,128]{3,1,2,0:T(8,128)(2,1)S(1)} %get-tuple-element.76), channel_id=1, source_target_pairs={{0,4},{4,8},{8,12},{12,16},{16,20},{20,24},{24,28},{28,0},{1,5},{5... | collective-permute-start | bytes 18440 | tf_op jit(solution)/shard_map/ppermute | solution.py:21
  108.0 5.0 %collective-permute-start.3 = (bf16[3,8,18,1]{3,1,2,0:T(8,128)(2,1)S(1)}, bf16[3,8,18,1]{3,1,2,0:T(8,128)(2,1)S(1)}, u32[]{:S(2)}, u32[]{:S(2)}) collective-permute-start(bf16[3,8,18,1]{3,1,2,0:T(8,128)(2,1)S(1)} %get-tuple-element.73), channel_id=1, source_target_pairs={{1,0},{2,1},{3,2},{0,3},{5,4},{6,5},{7,6},{4,7},{9,8},{10,9},{11,1... | collective-permute-start | bytes 2600 | tf_op jit(solution)/shard_map/ppermute | solution.py:22
  110.7 5.6 %collective-permute-start.2 = (bf16[3,8,18,1]{3,1,2,0:T(8,128)(2,1)S(1)}, bf16[3,8,18,1]{3,1,2,0:T(8,128)(2,1)S(1)}, u32[]{:S(2)}, u32[]{:S(2)}) collective-permute-start(bf16[3,8,18,1]{3,1,2,0:T(8,128)(2,1)S(1)} %get-tuple-element.72), channel_id=1, source_target_pairs={{0,1},{1,2},{2,3},{3,0},{4,5},{5,6},{6,7},{7,4},{8,9},{9,10},{10,1... | collective-permute-start | bytes 2600 | tf_op jit(solution)/shard_map/ppermute | solution.py:21
  152.7 7.8 %all-to-all-start.2 = ((bf16[4,2,128]{2,1,0:T(2,128)(2,1)}), bf16[4,2,128]{2,1,0:T(2,128)(2,1)S(1)}, u32[]{:S(2)}, u32[]{:S(2)}) async-start(bf16[4,2,128]{2,1,0:T(2,128)(2,1)} %copy.387), calls=%async_computation.3 | async-start | bytes 4096 | tf_op jit(solution)/shard_map/all_to_all | solution.py:164
  162.7 7.9 %all-to-all-start.3 = ((f32[4,1,256]{2,1,0:T(1,128)}), f32[4,1,256]{2,1,0:T(1,128)S(1)}, u32[]{:S(2)}, u32[]{:S(2)}) async-start(f32[4,1,256]{2,1,0:T(1,128)} %reshape.1014), calls=%async_computation.4 | async-start | bytes 8192 | tf_op jit(solution)/shard_map/all_to_all | solution.py:168
  166.0 33.2 %reduce-scatter.7.cloned.1.call-start = ((), (), s32[]{:S(2)}) async-start(), calls=%async_computation.7 | async-start | bytes 73728 | tf_op jit(solution)/shard_map/reduce_scatter | solution.py:177
  200.0 1.5 collective-permute-start.5
  200.2 4.9 %collective-permute-start.4 = (bf16[3,8,1,128]{3,1,2,0:T(8,128)(2,1)S(1)}, bf16[3,8,1,128]{3,1,2,0:T(8,128)(2,1)S(1)}, u32[]{:S(2)}, u32[]{:S(2)}) collective-permute-start(bf16[3,8,1,128]{3,1,2,0:T(8,128)(2,1)S(1)} %get-tuple-element.74), channel_id=1, source_target_pairs={{0,4},{4,8},{8,12},{12,16},{16,20},{20,24},{24,28},{28,0},{1,5},{5... | collective-permute-start | bytes 18440 | tf_op jit(solution)/shard_map/ppermute | solution.py:21
  205.2 5.0 %collective-permute-start.7 = (bf16[3,8,18,1]{3,1,2,0:T(8,128)(2,1)S(1)}, bf16[3,8,18,1]{3,1,2,0:T(8,128)(2,1)S(1)}, u32[]{:S(2)}, u32[]{:S(2)}) collective-permute-start(bf16[3,8,18,1]{3,1,2,0:T(8,128)(2,1)S(1)} %get-tuple-element.71), channel_id=1, source_target_pairs={{1,0},{2,1},{3,2},{0,3},{5,4},{6,5},{7,6},{4,7},{9,8},{10,9},{11,1... | collective-permute-start | bytes 2600 | tf_op jit(solution)/shard_map/ppermute | solution.py:22
  207.9 5.6 %collective-permute-start.6 = (bf16[3,8,18,1]{3,1,2,0:T(8,128)(2,1)S(1)}, bf16[3,8,18,1]{3,1,2,0:T(8,128)(2,1)S(1)}, u32[]{:S(2)}, u32[]{:S(2)}) collective-permute-start(bf16[3,8,18,1]{3,1,2,0:T(8,128)(2,1)S(1)} %get-tuple-element.70), channel_id=1, source_target_pairs={{0,1},{1,2},{2,3},{3,0},{4,5},{5,6},{6,7},{7,4},{8,9},{9,10},{10,1... | collective-permute-start | bytes 2600 | tf_op jit(solution)/shard_map/ppermute | solution.py:21
  (16 other events, 25.0 us)
Sparse Core Ops, SparseCore 0:
  75.7 26.3 reduce-scatter.4
  172.8 26.3 reduce-scatter.6
where the time goes:
time: 228 us; the launch traced here: 227 us
  waiting for transfers between devices  84.8 us (37%)
  blocking collectives  56.3 us (25%)
  starting transfers between devices  21 us (9%)
  local copies, waits for them, and re-layouts  17.1 us (8%)
  matrix products  16.9 us (7%)
  other arithmetic  15.9 us (7%)
  between operations  15.3 us (7%)
    unnamed x2, blocking collectives  56.3 us
    reduce_scatter x2, waiting for transfers between devices, surface_flux(): lax.psum_scatter(jnp.dot(table, flat_matched, precision=highest), 'tile',...  52.2 us
    ppermute x4, waiting for transfers between devices, padded_2(): before = lax.ppermute(last, axis, up)  13.6 us
    dot_general x30, matrix products, apply_along(): return jnp.einsum(formula, blocks, matrix, precision=highest).reshape(shape)  9.26 us
    all_to_all x2, waiting for transfers between devices, surface_flux(): lax.all_to_all(mapped, 'deg', split_axis=2, concat_axis=0, tiled=True)  8.98 us
    all_to_all x2, starting transfers between devices, surface_flux(): lax.all_to_all(mapped, 'deg', split_axis=2, concat_axis=0, tiled=True)  7.44 us
    all_to_all x2, starting transfers between devices, surface_flux(): lax.all_to_all(coeff.astype(jnp.bfloat16), 'deg', split_axis=0, concat_ax...  6.94 us
    unnamed x81, local copies, waits for them, and re-layouts  6.64 us
  transfers between devices with their start and end apart: 14, of which 13 were waited for; matrix products, arithmetic and copies ran while one was open for 7% of the time, Pallas kernels for 0%

commit v1 on v0

--- a/solution.py
+++ b/solution.py
@@ -9,6 +9,18 @@
 time_step = 0.01
 highest = lax.Precision.HIGHEST
 gll_interior = [0.2092992179024789, 0.5917001814331423, 0.8717401485096066]
+
+
+def in_blocks(x, dim, size):
+    shape = x.shape
+    blocks = x.reshape(*shape[:dim], size, shape[dim] // size, *shape[dim + 1 :])
+    return jnp.moveaxis(blocks, dim, 0)
+
+
+def in_order(pieces, dim):
+    pieces = jnp.moveaxis(pieces, 0, dim)
+    dims = pieces.shape
+    return pieces.reshape(*dims[:dim], dims[dim] * dims[dim + 1], *dims[dim + 2 :])
 
 
 def padded_2(value, sides, width):
@@ -165,7 +177,16 @@
             coeff.astype(jnp.bfloat16), "deg", split_axis=0, concat_axis=2, tiled=True
         )
         mapped = jnp.einsum("kpq,kcq->kcp", match_ops, owned, preferred_element_type=jnp.float32)
-        matched = lax.all_to_all(mapped, "deg", split_axis=2, concat_axis=0, tiled=True)
+        length_2, here = (lax.axis_size("deg"), lax.axis_index("deg"))
+        blocks_2 = in_blocks(mapped, 2, length_2)
+        gathered = [blocks_2[here]]
+        for step in range(1, length_2):
+            sent = blocks_2[here ^ step]
+            gathered.append(
+                lax.ppermute(sent, "deg", [(i_2, i_2 ^ step) for i_2 in range(length_2)])
+            )
+        blocks_2 = jnp.stack(gathered)[here ^ jnp.arange(length_2)]
+        matched = in_order(blocks_2, 0)
         my_waves = lax.dynamic_slice_in_dim(wave_of_slot, tile_index * per_tile, per_tile)
         flat_matched = matched.reshape(per_tile * 2, nb_dev)
         angle = phases(

time: 228 us -> 220 us (0.965)
  other arithmetic: 15.9 us -> 12.3 us
    all_to_all x2 -> x0, waiting for transfers between devices: 8.98 us -> none  [surface_flux(): lax.all_to_all(mapped, 'deg', split_axis=2, concat_axis=0, tiled=True)]
    all_to_all x2 -> x0, starting transfers between devices: 7.44 us -> none  [surface_flux(): lax.all_to_all(mapped, 'deg', split_axis=2, concat_axis=0, tiled=True)]
    ppermute x0 -> x6, starting transfers between devices: none -> 7.08 us  [surface_flux(): lax.ppermute(sent, 'deg', [(i_2, i_2 ^ step) for i_2 in range(length_2)])]
    ppermute x0 -> x6, waiting for transfers between devices: none -> 5.34 us  [surface_flux(): lax.ppermute(sent, 'deg', [(i_2, i_2 ^ step) for i_2 in range(length_2)])]
    unnamed x81 -> x80, local copies, waits for them, and re-layouts: 6.64 us -> 3.8 us
    unnamed x2 -> x0, other arithmetic: 2.44 us -> none
  transfers between devices with their start and end apart: 14 -> 18, of which waited for: 13 -> 16; matrix products, arithmetic and copies ran while one was open for 7% -> 7% of each run, Pallas kernels for 0% -> 0%
where the time goes in v1:
time: 220 us; the launch traced here: 219 us
  waiting for transfers between devices  82.7 us (38%)
  blocking collectives  56.3 us (26%)
  starting transfers between devices  20.8 us (9%)
  matrix products  16.8 us (8%)
  between operations  15.3 us (7%)
  local copies, waits for them, and re-layouts  15.2 us (7%)
  other arithmetic  12.3 us (6%)
    unnamed x2, blocking collectives  56.3 us
    reduce_scatter x2, waiting for transfers between devices, surface_flux(): lax.psum_scatter(jnp.dot(table, flat_matched, precision=highest), 'tile',...  54 us
    ppermute x4, waiting for transfers between devices, padded_2(): before = lax.ppermute(last, axis, up)  13.6 us
    dot_general x30, matrix products, apply_along(): return jnp.einsum(formula, blocks, matrix, precision=highest).reshape(shape)  9.27 us
    ppermute x6, starting transfers between devices, surface_flux(): lax.ppermute(sent, 'deg', [(i_2, i_2 ^ step) for i_2 in range(length_2)])  7.08 us
    all_to_all x2, starting transfers between devices, surface_flux(): lax.all_to_all(coeff.astype(jnp.bfloat16), 'deg', split_axis=0, concat_ax...  6.94 us
    ppermute x4, waiting for transfers between devices, padded_2(): after = lax.ppermute(first, axis, down)  6.38 us
    ppermute x4, starting transfers between devices, padded_2(): after = lax.ppermute(first, axis, down)  5.71 us
  transfers between devices with their start and end apart: 18, of which 16 were waited for; matrix products, arithmetic and copies ran while one was open for 7% of the time, Pallas kernels for 0%

profile of v1, /device:TPU:0, one launch (start us, length us, event | category | flops | bytes accessed | tf_op | source)
XLA Modules:
  0.0 219.3 jit_solution(14381756301650883284)
XLA Ops:
  10.2 1.0 fusion.112
  11.2 30.3 %all-reduce = bf16[32,2,128]{2,0,1:T(8,128)(2,1)S(1)} all-reduce(f32[32,2,128]{2,0,1:T(8,128)S(1)} %fusion.112), channel_id=2, replica_groups=mesh['tile'=8,'deg'=4] {'tile'}, use_global_device_ids=true, to_apply=%region_0.1.clone | all-reduce | flops 8192 | bytes 49152
  41.5 1.2 dynamic-slice.56
  43.9 3.7 %all-to-all-start = ((bf16[4,2,128]{2,1,0:T(2,128)(2,1)}), bf16[4,2,128]{2,1,0:T(2,128)(2,1)S(1)}, u32[]{:S(2)}, u32[]{:S(2)}) async-start(bf16[4,2,128]{2,1,0:T(2,128)(2,1)} %copy.328), calls=%async_computation | async-start | bytes 4096 | tf_op jit(solution)/shard_map/all_to_all | solution.py:176
  49.4 1.1 fusion.47
  50.5 1.0 convolution_bitcast_fusion.6
  51.6 0.9 fusion.176
  53.3 1.0 fusion.50
  62.1 2.9 %collective-permute-start.2 = (f32[1,2,128]{2,1,0:T(2,128)S(1)}, f32[1,2,128]{2,1,0:T(2,128)S(1)}, u32[]{:S(2)}, u32[]{:S(2)}) collective-permute-start(f32[1,2,128]{2,1,0:T(2,128)S(1)} %get-tuple-element.95), channel_id=1, source_target_pairs={{0,3},{1,2},{2,1},{3,0},{4,7},{5,6},{6,5},{7,4},{8,11},{9,10},{10,... | collective-permute-start | bytes 3080 | tf_op jit(solution)/shard_map/ppermute | solution.py:186
  66.6 2.0 collective-permute-done.1
  69.7 0.9 fusion.179
  71.3 26.8 %reduce-scatter.5.cloned.1.call-done = f32[16,128]{1,0:T(8,128)} async-done(((f32[128,128]{1,0:T(8,128)}), f32[16,128]{1,0:T(8,128)}) %reduce-scatter.5.cloned.1.call-update) | async-done | bytes 8208 | tf_op jit(solution)/shard_map/reduce_scatter | solution.py:198
  100.4 3.5 %collective-permute-done.3 = bf16[3,8,1,128]{3,1,2,0:T(8,128)(2,1)S(1)} collective-permute-done((bf16[3,8,1,128]{3,1,2,0:T(8,128)(2,1)S(1)}, bf16[3,8,1,128]{3,1,2,0:T(8,128)(2,1)S(1)}, u32[]{:S(2)}, u32[]{:S(2)}) %collective-permute-start.3) | collective-permute-done | bytes 6176 | tf_op jit(solution)/shard_map/ppermute | solution.py:33
  104.1 2.7 %collective-permute-start.6 = (bf16[3,8,18,1]{3,1,2,0:T(8,128)(2,1)S(1)}, bf16[3,8,18,1]{3,1,2,0:T(8,128)(2,1)S(1)}, u32[]{:S(2)}, u32[]{:S(2)}) collective-permute-start(bf16[3,8,18,1]{3,1,2,0:T(8,128)(2,1)S(1)} %get-tuple-element.73), channel_id=1, source_target_pairs={{1,0},{2,1},{3,2},{0,3},{5,4},{6,5},{7,6},{4,7},{9,8},{10,9},{11,1... | collective-permute-start | bytes 2600 | tf_op jit(solution)/shard_map/ppermute | solution.py:34
  106.8 2.2 %collective-permute-done.6 = bf16[3,8,18,1]{3,1,2,0:T(8,128)(2,1)S(1)} collective-permute-done((bf16[3,8,18,1]{3,1,2,0:T(8,128)(2,1)S(1)}, bf16[3,8,18,1]{3,1,2,0:T(8,128)(2,1)S(1)}, u32[]{:S(2)}, u32[]{:S(2)}) %collective-permute-start.6) | collective-permute-done | bytes 896 | tf_op jit(solution)/shard_map/ppermute | solution.py:34
  109.1 3.3 %collective-permute-done.5 = bf16[3,8,18,1]{3,1,2,0:T(8,128)(2,1)S(1)} collective-permute-done((bf16[3,8,18,1]{3,1,2,0:T(8,128)(2,1)S(1)}, bf16[3,8,18,1]{3,1,2,0:T(8,128)(2,1)S(1)}, u32[]{:S(2)}, u32[]{:S(2)}) %collective-permute-start.5) | collective-permute-done | bytes 896 | tf_op jit(solution)/shard_map/ppermute | solution.py:33
  113.7 1.3 slice.301
  116.0 2.0 maximum_bitcast_fusion
  122.1 26.0 %all-reduce.1 = bf16[32,2,128]{2,0,1:T(8,128)(2,1)S(1)} all-reduce(f32[32,2,128]{2,0,1:T(8,128)S(1)} %fusion.111), channel_id=4, replica_groups=mesh['tile'=8,'deg'=4] {'tile'}, use_global_device_ids=true, to_apply=%region_2.3.clone | all-reduce | flops 8192 | bytes 49152
  148.7 3.2 %all-to-all-start.1 = ((bf16[4,2,128]{2,1,0:T(2,128)(2,1)}), bf16[4,2,128]{2,1,0:T(2,128)(2,1)S(1)}, u32[]{:S(2)}, u32[]{:S(2)}) async-start(bf16[4,2,128]{2,1,0:T(2,128)(2,1)} %copy.379), calls=%async_computation.2 | async-start | bytes 4096 | tf_op jit(solution)/shard_map/all_to_all | solution.py:176
  153.2 3.3 %all-to-all-done.1 = bf16[4,2,128]{2,1,0:T(2,128)(2,1)S(1)} async-done(((bf16[4,2,128]{2,1,0:T(2,128)(2,1)}), bf16[4,2,128]{2,1,0:T(2,128)(2,1)S(1)}, u32[]{:S(2)}, u32[]{:S(2)}) %all-to-all-start.1) | async-done | bytes 2080 | tf_op jit(solution)/shard_map/all_to_all | solution.py:176
  157.3 1.5 collective-permute-start.8
  158.8 1.5 collective-permute-start.7
  161.2 1.1 collective-permute-done.7
  164.1 27.2 %reduce-scatter.7.cloned.1.call-done = f32[16,128]{1,0:T(8,128)} async-done(((f32[128,128]{1,0:T(8,128)}), f32[16,128]{1,0:T(8,128)}) %reduce-scatter.7.cloned.1.call-update) | async-done | bytes 8208 | tf_op jit(solution)/shard_map/reduce_scatter | solution.py:198
  192.7 0.9 collective-permute-done.11
  193.6 3.5 %collective-permute-done.10 = bf16[3,8,1,128]{3,1,2,0:T(8,128)(2,1)S(1)} collective-permute-done((bf16[3,8,1,128]{3,1,2,0:T(8,128)(2,1)S(1)}, bf16[3,8,1,128]{3,1,2,0:T(8,128)(2,1)S(1)}, u32[]{:S(2)}, u32[]{:S(2)}) %collective-permute-start.10) | collective-permute-done | bytes 6176 | tf_op jit(solution)/shard_map/ppermute | solution.py:33
  197.3 2.7 %collective-permute-start.13 = (bf16[3,8,18,1]{3,1,2,0:T(8,128)(2,1)S(1)}, bf16[3,8,18,1]{3,1,2,0:T(8,128)(2,1)S(1)}, u32[]{:S(2)}, u32[]{:S(2)}) collective-permute-start(bf16[3,8,18,1]{3,1,2,0:T(8,128)(2,1)S(1)} %get-tuple-element.71), channel_id=1, source_target_pairs={{1,0},{2,1},{3,2},{0,3},{5,4},{6,5},{7,6},{4,7},{9,8},{10,9},{11,1... | collective-permute-start | bytes 2600 | tf_op jit(solution)/shard_map/ppermute | solution.py:34
  200.0 2.3 %collective-permute-done.13 = bf16[3,8,18,1]{3,1,2,0:T(8,128)(2,1)S(1)} collective-permute-done((bf16[3,8,18,1]{3,1,2,0:T(8,128)(2,1)S(1)}, bf16[3,8,18,1]{3,1,2,0:T(8,128)(2,1)S(1)}, u32[]{:S(2)}, u32[]{:S(2)}) %collective-permute-start.13) | collective-permute-done | bytes 896 | tf_op jit(solution)/shard_map/ppermute | solution.py:34
  202.3 3.3 %collective-permute-done.12 = bf16[3,8,18,1]{3,1,2,0:T(8,128)(2,1)S(1)} collective-permute-done((bf16[3,8,18,1]{3,1,2,0:T(8,128)(2,1)S(1)}, bf16[3,8,18,1]{3,1,2,0:T(8,128)(2,1)S(1)}, u32[]{:S(2)}, u32[]{:S(2)}) %collective-permute-start.12) | collective-permute-done | bytes 896 | tf_op jit(solution)/shard_map/ppermute | solution.py:33
  206.9 1.3 slice.324
  209.2 2.0 maximum_bitcast_fusion.1
  (233 shorter events, 35.9 us)
Async XLA Ops:
  6.5 55.3 %copy-start = (bf16[1,512,512]{2,1,0:T(8,128)(2,1)S(1)}, bf16[1,512,512]{2,1,0:T(8,128)(2,1)}, u32[]{:S(2)}) copy-start(bf16[1,512,512]{2,1,0:T(8,128)(2,1)} %param.13) | copy-start | bytes 1572868
  7.3 90.8 %copy-start.30 = (f32[16]{0:T(128)}, f32[16]{0:T(128)S(1)}, u32[]{:S(2)}) copy-start(f32[16]{0:T(128)S(1)} %mul.669) | copy-start | bytes 196
  8.8 39.7 %copy-start.34 = (f32[16]{0:T(128)}, f32[16]{0:T(128)S(1)}, u32[]{:S(2)}) copy-start(f32[16]{0:T(128)S(1)} %get-tuple-element.103) | copy-start | bytes 196
  43.9 17.9 %all-to-all-start = ((bf16[4,2,128]{2,1,0:T(2,128)(2,1)}), bf16[4,2,128]{2,1,0:T(2,128)(2,1)S(1)}, u32[]{:S(2)}, u32[]{:S(2)}) async-start(bf16[4,2,128]{2,1,0:T(2,128)(2,1)} %copy.328), calls=%async_computation | async-start | bytes 4096 | tf_op jit(solution)/shard_map/all_to_all | solution.py:176
  47.7 50.4 %reduce-scatter.5.cloned.1.call-start = ((), (), s32[]{:S(2)}) async-start(), calls=%async_computation.4 | async-start | bytes 73728 | tf_op jit(solution)/shard_map/reduce_scatter | solution.py:198
  48.5 12.5 %copy-start.24 = (f32[8,2,8]{2,1,0:T(2,128)}, f32[8,2,8]{2,1,0:T(2,128)S(1)}, u32[]{:S(2)}) copy-start(f32[8,2,8]{2,1,0:T(2,128)S(1)} %broadcast_multiply_fusion.3) | copy-start | bytes 1540
  49.4 6.3 %copy-start.2 = (f32[3,8,16,128]{3,2,1,0:T(8,128)S(1)}, f32[3,8,16,128]{3,2,1,0:T(8,128)}, u32[]{:S(2)}) copy-start(f32[3,8,16,128]{3,2,1,0:T(8,128)} %param.12) | copy-start | bytes 589828
  49.4 6.5 %copy-start.1 = (f32[3,8,16,128]{3,2,1,0:T(8,128)S(1)}, f32[3,8,16,128]{3,2,1,0:T(8,128)}, u32[]{:S(2)}) copy-start(f32[3,8,16,128]{3,2,1,0:T(8,128)} %param.11) | copy-start | bytes 589828
  51.6 7.4 %copy-start.10 = (f32[8,16,128]{2,1,0:T(8,128)}, f32[8,16,128]{2,1,0:T(8,128)S(1)}, u32[]{:S(2)}) copy-start(f32[8,16,128]{2,1,0:T(8,128)S(1)} %convolution_bitcast_fusion.6) | copy-start | bytes 196612
  51.6 4.9 %copy-start.22 = (f32[8,8,1,1]{1,0,3,2:T(8,128)S(1)}, f32[8,8,1,1]{1,0,3,2:T(8,128)}, u32[]{:S(2)}) copy-start(f32[8,8,1,1]{1,0,3,2:T(8,128)} %constant.242) | copy-start | bytes 772
  56.5 14.2 %copy-start.6 = (f32[8,16,128]{2,1,0:T(8,128)}, f32[8,16,128]{2,1,0:T(8,128)S(1)}, u32[]{:S(2)}) copy-start(f32[8,16,128]{2,1,0:T(8,128)S(1)} %convolution_bitcast_fusion.9) | copy-start | bytes 196612
  56.7 14.0 %copy-start.12 = (f32[8,16,128]{2,1,0:T(8,128)}, f32[8,16,128]{2,1,0:T(8,128)S(1)}, u32[]{:S(2)}) copy-start(f32[8,16,128]{2,1,0:T(8,128)S(1)} %convolution_bitcast_fusion.10) | copy-start | bytes 196612
  57.5 4.0 %copy-start.8 = (f32[8,16,128]{2,1,0:T(8,128)}, f32[8,16,128]{2,1,0:T(8,128)S(1)}, u32[]{:S(2)}) copy-start(f32[8,16,128]{2,1,0:T(8,128)S(1)} %convolution_bitcast_fusion.13) | copy-start | bytes 196612
  59.7 11.0 %copy-start.18 = (f32[8,16,128]{2,0,1:T(8,128)}, f32[8,16,128]{2,0,1:T(8,128)S(1)}, u32[]{:S(2)}) copy-start(f32[8,16,128]{2,0,1:T(8,128)S(1)} %fusion.80) | copy-start | bytes 196612
  60.2 10.8 %copy-start.20 = (f32[8,16,128]{2,0,1:T(8,128)}, f32[8,16,128]{2,0,1:T(8,128)S(1)}, u32[]{:S(2)}) copy-start(f32[8,16,128]{2,0,1:T(8,128)S(1)} %fusion.86) | copy-start | bytes 196612
  62.1 4.5 %collective-permute-start.2 = (f32[1,2,128]{2,1,0:T(2,128)S(1)}, f32[1,2,128]{2,1,0:T(2,128)S(1)}, u32[]{:S(2)}, u32[]{:S(2)}) collective-permute-start(f32[1,2,128]{2,1,0:T(2,128)S(1)} %get-tuple-element.95), channel_id=1, source_target_pairs={{0,3},{1,2},{2,1},{3,0},{4,7},{5,6},{6,5},{7,4},{8,11},{9,10},{10,... | collective-permute-start | bytes 3080 | tf_op jit(solution)/shard_map/ppermute | solution.py:186
  65.0 3.6 %collective-permute-start.1 = (f32[1,2,128]{2,1,0:T(2,128)S(1)}, f32[1,2,128]{2,1,0:T(2,128)S(1)}, u32[]{:S(2)}, u32[]{:S(2)}) collective-permute-start(f32[1,2,128]{2,1,0:T(2,128)S(1)} %get-tuple-element.96), channel_id=1, source_target_pairs={{0,2},{1,3},{2,0},{3,1},{4,6},{5,7},{6,4},{7,5},{8,10},{9,11},{10,... | collective-permute-start | bytes 3080 | tf_op jit(solution)/shard_map/ppermute | solution.py:186
  65.6 3.6 %collective-permute-start = (f32[1,2,128]{2,1,0:T(2,128)S(1)}, f32[1,2,128]{2,1,0:T(2,128)S(1)}, u32[]{:S(2)}, u32[]{:S(2)}) collective-permute-start(f32[1,2,128]{2,1,0:T(2,128)S(1)} %get-tuple-element.97), channel_id=1, source_target_pairs={{0,1},{1,0},{2,3},{3,2},{4,5},{5,4},{6,7},{7,6},{8,9},{9,8},{10,11... | collective-permute-start | bytes 3080 | tf_op jit(solution)/shard_map/ppermute | solution.py:186
  98.9 1.5 collective-permute-start.4
  99.1 4.9 %collective-permute-start.3 = (bf16[3,8,1,128]{3,1,2,0:T(8,128)(2,1)S(1)}, bf16[3,8,1,128]{3,1,2,0:T(8,128)(2,1)S(1)}, u32[]{:S(2)}, u32[]{:S(2)}) collective-permute-start(bf16[3,8,1,128]{3,1,2,0:T(8,128)(2,1)S(1)} %get-tuple-element.76), channel_id=1, source_target_pairs={{0,4},{4,8},{8,12},{12,16},{16,20},{20,24},{24,28},{28,0},{1,5},{5... | collective-permute-start | bytes 18440 | tf_op jit(solution)/shard_map/ppermute | solution.py:33
  104.1 5.0 %collective-permute-start.6 = (bf16[3,8,18,1]{3,1,2,0:T(8,128)(2,1)S(1)}, bf16[3,8,18,1]{3,1,2,0:T(8,128)(2,1)S(1)}, u32[]{:S(2)}, u32[]{:S(2)}) collective-permute-start(bf16[3,8,18,1]{3,1,2,0:T(8,128)(2,1)S(1)} %get-tuple-element.73), channel_id=1, source_target_pairs={{1,0},{2,1},{3,2},{0,3},{5,4},{6,5},{7,6},{4,7},{9,8},{10,9},{11,1... | collective-permute-start | bytes 2600 | tf_op jit(solution)/shard_map/ppermute | solution.py:34
  106.8 5.6 %collective-permute-start.5 = (bf16[3,8,18,1]{3,1,2,0:T(8,128)(2,1)S(1)}, bf16[3,8,18,1]{3,1,2,0:T(8,128)(2,1)S(1)}, u32[]{:S(2)}, u32[]{:S(2)}) collective-permute-start(bf16[3,8,18,1]{3,1,2,0:T(8,128)(2,1)S(1)} %get-tuple-element.72), channel_id=1, source_target_pairs={{0,1},{1,2},{2,3},{3,0},{4,5},{5,6},{6,7},{7,4},{8,9},{9,10},{10,1... | collective-permute-start | bytes 2600 | tf_op jit(solution)/shard_map/ppermute | solution.py:33
  148.7 7.8 %all-to-all-start.1 = ((bf16[4,2,128]{2,1,0:T(2,128)(2,1)}), bf16[4,2,128]{2,1,0:T(2,128)(2,1)S(1)}, u32[]{:S(2)}, u32[]{:S(2)}) async-start(bf16[4,2,128]{2,1,0:T(2,128)(2,1)} %copy.379), calls=%async_computation.2 | async-start | bytes 4096 | tf_op jit(solution)/shard_map/all_to_all | solution.py:176
  151.9 39.3 %reduce-scatter.7.cloned.1.call-start = ((), (), s32[]{:S(2)}) async-start(), calls=%async_computation.5 | async-start | bytes 73728 | tf_op jit(solution)/shard_map/reduce_scatter | solution.py:198
  152.2 39.1 %copy-start.31 = (f32[16]{0:T(128)S(1)}, f32[16]{0:T(128)}, u32[]{:S(2)}) copy-start(f32[16]{0:T(128)} %copy-done.30) | copy-start | bytes 196
  156.7 4.5 %collective-permute-start.9 = (f32[1,2,128]{2,1,0:T(2,128)S(1)}, f32[1,2,128]{2,1,0:T(2,128)S(1)}, u32[]{:S(2)}, u32[]{:S(2)}) collective-permute-start(f32[1,2,128]{2,1,0:T(2,128)S(1)} %get-tuple-element.91), channel_id=1, source_target_pairs={{0,3},{1,2},{2,1},{3,0},{4,7},{5,6},{6,5},{7,4},{8,11},{9,10},{10,... | collective-permute-start | bytes 3080 | tf_op jit(solution)/shard_map/ppermute | solution.py:186
  157.3 3.9 %collective-permute-start.8 = (f32[1,2,128]{2,1,0:T(2,128)S(1)}, f32[1,2,128]{2,1,0:T(2,128)S(1)}, u32[]{:S(2)}, u32[]{:S(2)}) collective-permute-start(f32[1,2,128]{2,1,0:T(2,128)S(1)} %get-tuple-element.92), channel_id=1, source_target_pairs={{0,2},{1,3},{2,0},{3,1},{4,6},{5,7},{6,4},{7,5},{8,10},{9,11},{10,... | collective-permute-start | bytes 3080 | tf_op jit(solution)/shard_map/ppermute | solution.py:186
  158.8 3.6 %collective-permute-start.7 = (f32[1,2,128]{2,1,0:T(2,128)S(1)}, f32[1,2,128]{2,1,0:T(2,128)S(1)}, u32[]{:S(2)}, u32[]{:S(2)}) collective-permute-start(f32[1,2,128]{2,1,0:T(2,128)S(1)} %get-tuple-element.93), channel_id=1, source_target_pairs={{0,1},{1,0},{2,3},{3,2},{4,5},{5,4},{6,7},{7,6},{8,9},{9,8},{10,11... | collective-permute-start | bytes 3080 | tf_op jit(solution)/shard_map/ppermute | solution.py:186
  192.1 1.5 collective-permute-start.11
  192.3 4.9 %collective-permute-start.10 = (bf16[3,8,1,128]{3,1,2,0:T(8,128)(2,1)S(1)}, bf16[3,8,1,128]{3,1,2,0:T(8,128)(2,1)S(1)}, u32[]{:S(2)}, u32[]{:S(2)}) collective-permute-start(bf16[3,8,1,128]{3,1,2,0:T(8,128)(2,1)S(1)} %get-tuple-element.74), channel_id=1, source_target_pairs={{0,4},{4,8},{8,12},{12,16},{16,20},{20,24},{24,28},{28,0},{1,5},{5... | collective-permute-start | bytes 18440 | tf_op jit(solution)/shard_map/ppermute | solution.py:33
  197.3 5.0 %collective-permute-start.13 = (bf16[3,8,18,1]{3,1,2,0:T(8,128)(2,1)S(1)}, bf16[3,8,18,1]{3,1,2,0:T(8,128)(2,1)S(1)}, u32[]{:S(2)}, u32[]{:S(2)}) collective-permute-start(bf16[3,8,18,1]{3,1,2,0:T(8,128)(2,1)S(1)} %get-tuple-element.71), channel_id=1, source_target_pairs={{1,0},{2,1},{3,2},{0,3},{5,4},{6,5},{7,6},{4,7},{9,8},{10,9},{11,1... | collective-permute-start | bytes 2600 | tf_op jit(solution)/shard_map/ppermute | solution.py:34
  200.0 5.6 %collective-permute-start.12 = (bf16[3,8,18,1]{3,1,2,0:T(8,128)(2,1)S(1)}, bf16[3,8,18,1]{3,1,2,0:T(8,128)(2,1)S(1)}, u32[]{:S(2)}, u32[]{:S(2)}) collective-permute-start(bf16[3,8,18,1]{3,1,2,0:T(8,128)(2,1)S(1)} %get-tuple-element.70), channel_id=1, source_target_pairs={{0,1},{1,2},{2,3},{3,0},{4,5},{5,6},{6,7},{7,4},{8,9},{9,10},{10,1... | collective-permute-start | bytes 2600 | tf_op jit(solution)/shard_map/ppermute | solution.py:33
  (22 other events, 45.6 us)
Sparse Core Ops, SparseCore 0:
  70.8 27.2 reduce-scatter.4
  164.0 27.2 reduce-scatter.6
